TPU v7x, 32 devices: a whole 2x2x4 slice. The times are simulated.
32 devices in a mesh: ctx: 2 (over x), req: 4 (over y, core), mp: 4 (over z).
Axes of the slice: x: 2, y: 2, z: 4, core: 2. Of those that a mesh axis runs over, the one named last changes fastest.
Arguments:
- activations: bfloat16 [4, 256, 8192], P('req', 'ctx', 'mp'), may hold values from -6 to 6
- query_base: bfloat16 [4, 256, 8192], P('req', 'ctx', 'mp'), may hold values from -9 to 9
- key_base: bfloat16 [4, 256, 1024], P('req', 'ctx', 'mp'), may hold values from -9 to 9
- plain_value_rows: bfloat16 [4, 256, 1024], P('req', 'ctx', 'mp'), may hold values from -6 to 6
- query_down: bfloat16 [8, 64, 8192], P('req', 'ctx', 'mp'), may hold values from -0.0625 to 0.0625
- query_up: bfloat16 [8, 64, 8192], P('req', 'ctx', 'mp'), may hold values from -0.75 to 0.75
- value_down: bfloat16 [8, 64, 8192], P('req', 'ctx', 'mp'), may hold values from -0.0625 to 0.0625
- value_raise_factor: bfloat16 [8, 64, 1024], P('req', 'ctx', 'mp'), may hold values from -0.75 to 0.75
- member_lists: int32 [4, 2], P('req'), may hold values from 0 to 7
- prompt_lengths: int32 [4], P('req'), may hold values from 32 to 256, as said below
Outputs:
- attended: bfloat16 [2, 4, 256, 8192], P(None, 'req', 'ctx', 'mp')
Inputs may be any that keep to these rules, and one draw needn't show every extreme that they name: `prompt_lengths`: at least one prompt has all 256 positions live.
All inputs are finite; a program needn't handle non-finite values.
Results may differ from a plain program's by a relative error of at most 0.008.
Values may be sent and summed in bfloat16 or wider, within the bound.
No kernel may reach another device: no remote copies, remote signals or barrier semaphores. Data moves between devices by JAX's collectives and lax.ppermute only.
A program may use at most 64 MiB of HBM per device.

v0:
```python
import math
import jax
import jax.numpy as jnp
from jax import lax
from jax.sharding import PartitionSpec as P

HEAD_SIZE = 128


def block_rows(total_rows):
    if total_rows <= 512:
        return total_rows
    for candidate in range(512, 0, -1):
        if total_rows % candidate == 0:
            return candidate
    return total_rows


def select_members(factor_set, member_ids, member_count):
    onehot = (member_ids[:, None] == jnp.arange(member_count, dtype=jnp.int32)[None, :]).astype(
        jnp.bfloat16
    )
    return tuple(
        (
            jnp.einsum("sm,mkc->skc", onehot, factor, preferred_element_type=jnp.float32).astype(
                jnp.bfloat16
            )
            for factor in factor_set
        )
    )


def per_device(
    activations,
    query_base,
    key_base,
    plain_value_rows,
    query_down,
    query_up,
    value_down,
    value_raise_factor,
    member_lists,
    prompt_lengths,
):
    row_count = activations.shape[1]
    member_count = query_down.shape[0] * lax.axis_size("req")
    member_ids = member_lists[0]
    full_rank = (
        lax.all_gather(query_down, "ctx", axis=1, tiled=True),
        lax.all_gather(query_up, "ctx", axis=1, tiled=True),
        lax.all_gather(value_down, "ctx", axis=1, tiled=True),
        lax.all_gather(value_raise_factor, "ctx", axis=1, tiled=True),
    )
    all_members = (
        lax.all_gather(full_rank[0], "req", axis=0, tiled=True),
        lax.all_gather(full_rank[1], "req", axis=0, tiled=True),
        lax.all_gather(full_rank[2], "req", axis=0, tiled=True),
        lax.all_gather(full_rank[3], "req", axis=0, tiled=True),
    )
    chosen = select_members(all_members, member_ids, member_count)
    down_query, up_query, down_value, up_value = chosen
    tokens = activations[0]
    rank_query = jnp.einsum("rd,skd->rsk", tokens, down_query, preferred_element_type=jnp.float32)
    rank_value = jnp.einsum("rd,skd->rsk", tokens, down_value, preferred_element_type=jnp.float32)
    rank_query, rank_value = lax.psum((rank_query, rank_value), "mp")
    rank_query = rank_query.astype(jnp.bfloat16)
    rank_value = rank_value.astype(jnp.bfloat16)
    query_matrix = (
        query_base[0][:, None, :]
        + jnp.einsum("rsk,skc->rsc", rank_query, up_query, preferred_element_type=jnp.float32)
    ).astype(jnp.bfloat16)
    slot_count = query_matrix.shape[1]
    rank_width = rank_value.shape[2]
    group_count = key_base.shape[2] // HEAD_SIZE
    group_portion = query_matrix.shape[2] // (group_count * HEAD_SIZE)
    grouped = query_matrix.reshape(row_count, slot_count, group_count, group_portion, HEAD_SIZE)
    rows_of_keys = key_base[0]
    positions = lax.axis_index("ctx") * row_count + jnp.arange(row_count, dtype=jnp.int32)
    live_length = prompt_lengths[0]
    inverse = 1.0 / math.sqrt(HEAD_SIZE)

    def update(running, key_block, value_block, key_start):
        run_max, run_total, accumulated = running
        block_length = key_block.shape[0]
        heads_of_keys = key_block.reshape(block_length, group_count, HEAD_SIZE)
        heads_of_values = value_block.reshape(block_length, slot_count, group_count, HEAD_SIZE)
        scores = (
            jnp.einsum(
                "rsgjd,kgd->sgjrk", grouped, heads_of_keys, preferred_element_type=jnp.float32
            )
            * inverse
        )
        key_positions = key_start + jnp.arange(block_length, dtype=jnp.int32)
        visible = (key_positions[None, :] <= positions[:, None]) & (
            key_positions[None, :] < live_length
        )
        masked = jnp.where(visible, scores, -1e30)
        new_max = jnp.maximum(run_max, jnp.max(masked, axis=-1))
        weights = jnp.where(visible, jnp.exp(masked - new_max[..., None]), 0.0)
        factor = jnp.exp(run_max - new_max)
        new_total = run_total * factor + jnp.sum(weights, axis=-1)
        new_accumulated = accumulated * factor[..., None] + jnp.einsum(
            "sgjrk,ksgd->sgjrd",
            weights.astype(jnp.bfloat16),
            heads_of_values,
            preferred_element_type=jnp.float32,
        )
        return (new_max, new_total, new_accumulated)

    initial = (
        jnp.full((slot_count, group_count, group_portion, row_count), -1e30, jnp.float32),
        jnp.zeros((slot_count, group_count, group_portion, row_count), jnp.float32),
        jnp.zeros((slot_count, group_count, group_portion, row_count, HEAD_SIZE), jnp.float32),
    )
    base_rows = plain_value_rows[0]
    piece_rows = base_rows.shape[0]
    ranks = rank_value.reshape(row_count, slot_count * rank_width).reshape(
        piece_rows, slot_count, rank_width
    )
    built = (
        base_rows[:, None, :]
        + jnp.einsum("rsk,skc->rsc", ranks, up_value, preferred_element_type=jnp.float32)
    ).astype(jnp.bfloat16)
    packed = built.reshape(piece_rows, slot_count * group_count * HEAD_SIZE)
    key_piece = lax.all_gather(rows_of_keys, "ctx", axis=0, tiled=True)
    value_piece = lax.all_gather(packed, "ctx", axis=0, tiled=True)
    first_row = jnp.int32(0)
    piece_rows = key_piece.shape[0]
    step_rows = block_rows(piece_rows)

    def advance(block_index, current):
        offset = block_index * step_rows
        key_block = lax.dynamic_slice_in_dim(key_piece, offset, step_rows, 0)
        value_block = lax.dynamic_slice_in_dim(value_piece, offset, step_rows, 0)
        key_start = first_row + offset
        return update(current, key_block, value_block, key_start)

    run_max, run_total, accumulated = lax.fori_loop(0, piece_rows // step_rows, advance, initial)
    result = accumulated / run_total[..., None]
    result = (
        jnp.transpose(result, (0, 3, 1, 2, 4))
        .reshape(slot_count, row_count, group_count * group_portion * HEAD_SIZE)
        .astype(jnp.bfloat16)
    )
    return result[:, None]


def solution(mesh):
    in_specs = (
        P("req", "ctx", "mp"),
        P("req", "ctx", "mp"),
        P("req", "ctx", "mp"),
        P("req", "ctx", "mp"),
        P("req", "ctx", "mp"),
        P("req", "ctx", "mp"),
        P("req", "ctx", "mp"),
        P("req", "ctx", "mp"),
        P("req", None),
        P("req"),
    )
    out_specs = P(None, "req", "ctx", "mp")
    return jax.shard_map(
        per_device, mesh=mesh, in_specs=in_specs, out_specs=out_specs, check_vma=False
    )
```

profile of v0, /device:TPU:0, one launch (start us, length us, event | category | flops | bytes accessed | tf_op | source)
XLA Modules:
  0.0 111.7 jit_solution(13145723315272196515)
XLA Ops:
  6.5 12.0 %all_gather.37 = bf16[2,64,2048]{2,1,0:T(8,128)(2,1)} all-gather(bf16[2,32,2048]{2,1,0:T(8,128)(2,1)} %param.16), channel_id=1, replica_groups=mesh['ctx'=2,'req'=4,'mp'=4] {'ctx'}, dimensions={1}, use_global_device_ids=true | all-gather | bytes 786432 | tf_op jit(solution)/shard_map/all_gather | solution.py:51
  18.6 0.0 all-gather.9.cloned.1.call-update
  18.6 0.0 all-gather.7.cloned.1.call-start
  18.6 8.5 %all_gather.32 = bf16[2,64,2048]{2,1,0:T(8,128)(2,1)} all-gather(bf16[2,32,2048]{2,1,0:T(8,128)(2,1)} %param.14), channel_id=1, replica_groups=mesh['ctx'=2,'req'=4,'mp'=4] {'ctx'}, dimensions={1}, use_global_device_ids=true | all-gather | bytes 786432 | tf_op jit(solution)/shard_map/all_gather | solution.py:49
  27.1 0.0 all-gather.5.cloned.1.call-start
  27.2 7.9 %all_gather.30 = bf16[2,64,2048]{2,1,0:T(8,128)(2,1)} all-gather(bf16[2,32,2048]{2,1,0:T(8,128)(2,1)S(1)} %copy-done.2), channel_id=1, replica_groups=mesh['ctx'=2,'req'=4,'mp'=4] {'ctx'}, dimensions={1}, use_global_device_ids=true | all-gather | bytes 786432 | tf_op jit(solution)/shard_map/all_gather | solution.py:50
  35.0 0.0 all-gather.5.cloned.1.call-update
  35.1 0.1 bitcast_convert_fusion
  35.2 0.3 copy.27
  36.2 0.1 copy.32
  36.4 0.1 copy.36
  36.5 4.6 %all_gather.35 = bf16[2,64,256]{2,1,0:T(8,128)(2,1)S(1)} all-gather(bf16[2,32,256]{2,1,0:T(8,128)(2,1)S(1)} %copy-done.5), channel_id=1, replica_groups=mesh['ctx'=2,'req'=4,'mp'=4] {'ctx'}, dimensions={1}, use_global_device_ids=true | all-gather | bytes 98304 | tf_op jit(solution)/shard_map/all_gather | solution.py:52
  41.0 5.0 %all-gather = bf16[1,256,256]{1,2,0:T(8,128)(2,1)S(1)} all-gather(bf16[1,128,256]{1,2,0:T(8,128)(2,1)S(1)} %copy.32), channel_id=2, replica_groups=mesh['ctx'=2,'req'=4,'mp'=4] {'ctx'}, dimensions={1}, use_global_device_ids=true | all-gather | bytes 196608 | tf_op jit(solution)/shard_map/all_gather | solution.py:125
  46.0 6.0 %all_gather.36 = bf16[8,64,256]{2,1,0:T(8,128)(2,1)S(1)} all-gather(bf16[2,64,256]{2,1,0:T(8,128)(2,1)S(1)} %all_gather.35), channel_id=1, replica_groups=mesh['ctx'=2,'req'=4,'mp'=4] {'req'}, dimensions={0}, use_global_device_ids=true | all-gather | bytes 327680 | tf_op jit(solution)/shard_map/all_gather | solution.py:58
  52.0 0.1 fusion.25
  52.1 0.3 convolution_convert_fusion.3
  52.4 0.0 all-gather.9.cloned.1.call-done
  52.5 3.1 %convolution_convert_fusion = bf16[2,64,2048]{2,0,1:T(2,128)(2,1)S(1)} fusion(bf16[8,64,2048]{2,1,0:T(8,128)(2,1)} %all-gather.9.cloned.1.call-done, s32[2]{0:T(128)S(1)} %bitcast.86), kind=kOutput, calls=%fused_computation.10 | convolution fusion | flops 4456464 | bytes 2621448 | tf_op jit(solution)/shard_map/sm,mkc->skc/dot_general | solution.py:25
  55.6 0.4 convolution_bitcast_fusion.2
  56.0 9.8 %all-gather.7.cloned.1.call-done = bf16[8,64,2048]{2,1,0:T(8,128)(2,1)} async-done(((bf16[2,64,2048]{2,1,0:T(8,128)(2,1)}), bf16[8,64,2048]{2,1,0:T(8,128)(2,1)}) %all-gather.7.cloned.1.call-update) | async-done | bytes 2097168 | tf_op jit(solution)/shard_map/all_gather | solution.py:55
  65.8 3.1 %convolution_convert_fusion.1 = bf16[2,64,2048]{2,0,1:T(2,128)(2,1)S(1)} fusion(bf16[8,64,2048]{2,1,0:T(8,128)(2,1)} %all-gather.7.cloned.1.call-done, s32[2]{0:T(128)S(1)} %bitcast.87), kind=kOutput, calls=%fused_computation.11 | convolution fusion | flops 4456464 | bytes 2621448 | tf_op jit(solution)/shard_map/sm,mkc->skc/dot_general | solution.py:25
  68.9 0.4 convolution_bitcast_fusion.3
  69.3 21.2 %all-reduce.2 = (bf16[128,2,64]{0,2,1:T(8,128)(2,1)S(1)}, bf16[128,2,64]{0,2,1:T(8,128)(2,1)S(1)}) all-reduce(f32[128,2,64]{0,2,1:T(8,128)S(1)} %convolution_bitcast_fusion.2, f32[128,2,64]{0,2,1:T(8,128)S(1)} %convolution_bitcast_fusion.3), channel_id=1, replica_groups=mesh['ctx'=2,'req'=4,'mp'=4] {'mp'}, use_global_device_ids=true, to_apply=%region_2.3 | all-reduce | flops 32768 | bytes 196608 | tf_op jit(solution)/shard_map/psum | solution.py:65
  90.5 0.0 all-gather.5.cloned.1.call-done
  90.5 3.1 %convolution_convert_fusion.2 = bf16[2,64,2048]{2,0,1:T(2,128)(2,1)S(1)} fusion(bf16[8,64,2048]{2,1,0:T(8,128)(2,1)} %all-gather.5.cloned.1.call-done, s32[2]{0:T(128)S(1)} %bitcast.88), kind=kOutput, calls=%fused_computation.12 | convolution fusion | flops 4456464 | bytes 2621448 | tf_op jit(solution)/shard_map/sm,mkc->skc/dot_general | solution.py:25
  93.7 0.6 fusion.5
  94.2 1.0 bitcast_reduce_fusion
  95.3 1.7 %fusion.2 = (f32[2,2,8,128]{3,2,0,1:T(8,128)S(1)}, bf16[2,2,8,128,256]{4,3,2,0,1:T(8,128)(2,1)S(1)}) fusion(f32[2,128,2,8,256]{4,1,3,2,0:T(8,128)S(1)} %get-tuple-element.40, f32[2,2,8,128]{3,2,0,1:T(8,128)S(1)} %get-tuple-element.28, pred[128,256]{1,0:T(8,128)(4,1)S(1)} %fusion.25), kind=kLoop, calls=%fused_computation.5 | loop fusion | flops 6287360 | bytes 6356992 | tf_op jit(solution)/shard_map/while/body/eval_jaxpr/reduce_sum | solution.py:101
  97.0 0.2 fusion.16
  97.3 5.8 %all_gather.39 = bf16[256,512]{0,1:T(8,128)(2,1)S(1)} all-gather(bf16[128,512]{0,1:T(8,128)(2,1)S(1)} %bitcast.83), channel_id=1, replica_groups=mesh['ctx'=2,'req'=4,'mp'=4] {'ctx'}, dimensions={0}, use_global_device_ids=true | all-gather | bytes 393216 | tf_op jit(solution)/shard_map/all_gather | solution.py:126
  103.1 0.8 fusion.7
  103.9 1.3 %copy.43 = bf16[2,1,128,2048]{3,2,1,0:T(8,128)(2,1)} copy(bf16[2,1,128,2048]{2,3,0,1:T(8,128)(2,1)S(1)} %bitcast.81) | data formatting | bytes 2097152 | tf_op jit(solution)/shard_map/convert_element_type | solution.py:143
  (21 shorter events, 0.1 us)
Async XLA Ops:
  6.5 49.1 %copy-start = (bf16[1,128,2048]{2,1,0:T(8,128)(2,1)S(1)}, bf16[1,128,2048]{2,1,0:T(8,128)(2,1)}, u32[]{:S(2)}) copy-start(bf16[1,128,2048]{2,1,0:T(8,128)(2,1)} %param.10) | copy-start | bytes 1572868
  6.5 20.6 %copy-start.2 = (bf16[2,32,2048]{2,1,0:T(8,128)(2,1)S(1)}, bf16[2,32,2048]{2,1,0:T(8,128)(2,1)}, u32[]{:S(2)}) copy-start(bf16[2,32,2048]{2,1,0:T(8,128)(2,1)} %param.15) | copy-start | bytes 786436
  6.5 28.5 %copy-start.1 = (bf16[1,128,2048]{2,1,0:T(8,128)(2,1)S(1)}, bf16[1,128,2048]{2,1,0:T(8,128)(2,1)}, u32[]{:S(2)}) copy-start(bf16[1,128,2048]{2,1,0:T(8,128)(2,1)} %param.11) | copy-start | bytes 1572868
  6.5 45.9 %all-gather.9.cloned.1.call-start = ((), (), s32[]{:S(2)}) async-start(), calls=%async_computation.2 | async-start | bytes 2621440 | tf_op jit(solution)/shard_map/all_gather | solution.py:57
  18.6 47.2 %all-gather.7.cloned.1.call-start = ((), (), s32[]{:S(2)}) async-start(), calls=%async_computation.1 | async-start | bytes 2621440 | tf_op jit(solution)/shard_map/all_gather | solution.py:55
  27.1 63.4 %all-gather.5.cloned.1.call-start = ((), (), s32[]{:S(2)}) async-start(), calls=%async_computation | async-start | bytes 2621440 | tf_op jit(solution)/shard_map/all_gather | solution.py:56
  35.0 1.2 %copy-start.4 = (bf16[1,128,256]{2,1,0:T(8,128)(2,1)S(1)}, bf16[1,128,256]{2,1,0:T(8,128)(2,1)}, u32[]{:S(2)}) copy-start(bf16[1,128,256]{2,1,0:T(8,128)(2,1)} %param.12) | copy-start | bytes 196612
  35.0 1.3 %copy-start.3 = (bf16[1,128,256]{2,1,0:T(8,128)(2,1)S(1)}, bf16[1,128,256]{2,1,0:T(8,128)(2,1)}, u32[]{:S(2)}) copy-start(bf16[1,128,256]{2,1,0:T(8,128)(2,1)} %param.13) | copy-start | bytes 196612
  35.1 1.4 %copy-start.5 = (bf16[2,32,256]{2,1,0:T(8,128)(2,1)S(1)}, bf16[2,32,256]{2,1,0:T(8,128)(2,1)}, u32[]{:S(2)}) copy-start(bf16[2,32,256]{2,1,0:T(8,128)(2,1)} %param.17) | copy-start | bytes 98308
  35.1 17.0 %copy-start.6 = (s32[1,2]{1,0:T(1,128)S(1)}, s32[1,2]{1,0:T(1,128)}, u32[]{:S(2)}) copy-start(s32[1,2]{1,0:T(1,128)} %param.18) | copy-start | bytes 28
Sparse Core Ops, SparseCore 0:
  18.7 22.8 all-gather.8
  43.2 22.5 all-gather.6
  67.4 22.5 all-gather.4
where the time goes:
time: 112 us
  blocking collectives  70.8 us (63%)
  between operations  14 us (12%)
  matrix products  13.1 us (12%)
  waiting for transfers between devices  9.9 us (9%)
  other arithmetic  1.96 us (2%)
  local copies, waits for them, and re-layouts  1.87 us (2%)
    psum x1, blocking collectives, per_device(): rank_query, rank_value = lax.psum((rank_query, rank_value), 'mp')  21.2 us
    all_gather x1, blocking collectives, per_device(): lax.all_gather(value_down, 'ctx', axis=1, tiled=True)  12 us
    all_gather x1, waiting for transfers between devices, per_device(): lax.all_gather(full_rank[0], 'req', axis=0, tiled=True)  9.81 us
    dot_general x4, matrix products, select_members(): jnp.einsum('sm,mkc->skc', onehot, factor, preferred_element_type=jnp.floa...  9.69 us
    all_gather x1, blocking collectives, per_device(): lax.all_gather(query_down, 'ctx', axis=1, tiled=True)  8.45 us
    all_gather x1, blocking collectives, per_device(): lax.all_gather(query_up, 'ctx', axis=1, tiled=True)  7.85 us
    all_gather x1, blocking collectives, per_device(): lax.all_gather(full_rank[3], 'req', axis=0, tiled=True)  6.01 us
    all_gather x1, blocking collectives, per_device(): value_piece = lax.all_gather(packed, 'ctx', axis=0, tiled=True)  5.77 us
  transfers between devices with their start and end apart: 3, of which 1 were waited for; matrix products, arithmetic and copies ran while one was open for 7% of the time, Pallas kernels for 0%

commit v1 on v0

--- a/solution.py
+++ b/solution.py
@@ -122,8 +122,11 @@
         + jnp.einsum("rsk,skc->rsc", ranks, up_value, preferred_element_type=jnp.float32)
     ).astype(jnp.bfloat16)
     packed = built.reshape(piece_rows, slot_count * group_count * HEAD_SIZE)
-    key_piece = lax.all_gather(rows_of_keys, "ctx", axis=0, tiled=True)
-    value_piece = lax.all_gather(packed, "ctx", axis=0, tiled=True)
+    key_piece, value_piece = jnp.split(
+        lax.all_gather(jnp.concatenate([rows_of_keys, packed], axis=1), "ctx", axis=0, tiled=True),
+        [rows_of_keys.shape[1]],
+        axis=1,
+    )
     first_row = jnp.int32(0)
     piece_rows = key_piece.shape[0]
     step_rows = block_rows(piece_rows)

time: 112 us -> 112 us (level)
  waiting for transfers between devices: 9.9 us -> 14.6 us
  blocking collectives: 70.8 us -> 66.5 us
    all_gather x1, waiting for transfers between devices: 0.02 us -> 14.5 us  [per_device(): lax.all_gather(full_rank[2], 'req', axis=0, tiled=True)]
    all_gather x1, waiting for transfers between devices: 9.81 us -> 0.02 us  [per_device(): lax.all_gather(full_rank[0], 'req', axis=0, tiled=True)]
    all_gather x2 -> x1, blocking collectives: 10.7 us -> 6.37 us  [per_device(): lax.all_gather(jnp.concatenate([rows_of_keys, packed], axis=1), 'ctx', ax...]
    all_gather x1, blocking collectives: 12 us -> 8.45 us  [per_device(): lax.all_gather(value_down, 'ctx', axis=1, tiled=True)]
    all_gather x1, blocking collectives: 8.45 us -> 12 us  [per_device(): lax.all_gather(query_down, 'ctx', axis=1, tiled=True)]
where the time goes in v1:
time: 112 us
  blocking collectives  66.5 us (59%)
  waiting for transfers between devices  14.6 us (13%)
  between operations  14 us (12%)
  matrix products  12.7 us (11%)
  local copies, waits for them, and re-layouts  2.05 us (2%)
  other arithmetic  1.54 us (1%)
    psum x1, blocking collectives, per_device(): rank_query, rank_value = lax.psum((rank_query, rank_value), 'mp')  21.2 us
    all_gather x1, waiting for transfers between devices, per_device(): lax.all_gather(full_rank[2], 'req', axis=0, tiled=True)  14.5 us
    all_gather x1, blocking collectives, per_device(): lax.all_gather(query_down, 'ctx', axis=1, tiled=True)  12 us
    dot_general x4, matrix products, select_members(): jnp.einsum('sm,mkc->skc', onehot, factor, preferred_element_type=jnp.floa...  9.86 us
    all_gather x1, blocking collectives, per_device(): lax.all_gather(value_down, 'ctx', axis=1, tiled=True)  8.45 us
    all_gather x1, blocking collectives, per_device(): lax.all_gather(query_up, 'ctx', axis=1, tiled=True)  7.85 us
    all_gather x1, blocking collectives, per_device(): lax.all_gather(jnp.concatenate([rows_of_keys, packed], axis=1), 'ctx', ax...  6.37 us
    all_gather x1, blocking collectives, per_device(): lax.all_gather(full_rank[3], 'req', axis=0, tiled=True)  6.03 us
  transfers between devices with their start and end apart: 3, of which 1 were waited for; matrix products, arithmetic and copies ran while one was open for 7% of the time, Pallas kernels for 0%

profile of v1, /device:TPU:0, one launch (start us, length us, event | category | flops | bytes accessed | tf_op | source)
XLA Modules:
  0.0 111.5 jit_solution(11985317121509348231)
XLA Ops:
  6.5 0.0 all-gather.8.cloned.1.call-start
  6.6 12.0 %all_gather.34 = bf16[2,64,2048]{2,1,0:T(8,128)(2,1)} all-gather(bf16[2,32,2048]{2,1,0:T(8,128)(2,1)} %param.14), channel_id=1, replica_groups=mesh['ctx'=2,'req'=4,'mp'=4] {'ctx'}, dimensions={1}, use_global_device_ids=true | all-gather | bytes 786432 | tf_op jit(solution)/shard_map/all_gather | solution.py:49
  18.6 0.0 all-gather.4.cloned.1.call-start
  18.7 8.5 %all_gather.29 = bf16[2,64,2048]{2,1,0:T(8,128)(2,1)} all-gather(bf16[2,32,2048]{2,1,0:T(8,128)(2,1)} %param.16), channel_id=1, replica_groups=mesh['ctx'=2,'req'=4,'mp'=4] {'ctx'}, dimensions={1}, use_global_device_ids=true | all-gather | bytes 786432 | tf_op jit(solution)/shard_map/all_gather | solution.py:51
  27.2 0.0 all-gather.6.cloned.1.call-start
  27.2 7.9 %all_gather.32 = bf16[2,64,2048]{2,1,0:T(8,128)(2,1)} all-gather(bf16[2,32,2048]{2,1,0:T(8,128)(2,1)S(1)} %copy-done.3), channel_id=1, replica_groups=mesh['ctx'=2,'req'=4,'mp'=4] {'ctx'}, dimensions={1}, use_global_device_ids=true | all-gather | bytes 786432 | tf_op jit(solution)/shard_map/all_gather | solution.py:50
  35.1 0.0 all-gather.6.cloned.1.call-update
  35.8 0.1 copy.28
  35.9 0.1 copy.29
  36.0 0.1 bitcast_convert_fusion
  36.2 0.3 copy.34
  36.5 0.2 copy-done.6
  36.7 4.6 %all_gather.27 = bf16[2,64,256]{2,1,0:T(8,128)(2,1)S(1)} all-gather(bf16[2,32,256]{2,1,0:T(8,128)(2,1)S(1)} %copy-done.6), channel_id=1, replica_groups=mesh['ctx'=2,'req'=4,'mp'=4] {'ctx'}, dimensions={1}, use_global_device_ids=true | all-gather | bytes 98304 | tf_op jit(solution)/shard_map/all_gather | solution.py:52
  41.2 6.0 %all_gather.28 = bf16[8,64,256]{2,1,0:T(8,128)(2,1)S(1)} all-gather(bf16[2,64,256]{2,1,0:T(8,128)(2,1)S(1)} %all_gather.27), channel_id=1, replica_groups=mesh['ctx'=2,'req'=4,'mp'=4] {'req'}, dimensions={0}, use_global_device_ids=true | all-gather | bytes 327680 | tf_op jit(solution)/shard_map/all_gather | solution.py:58
  47.3 0.1 fusion.24
  47.4 0.3 convolution_convert_fusion.3
  47.7 0.0 all-gather.8.cloned.1.call-done
  47.7 3.2 %convolution_convert_fusion = bf16[2,64,2048]{2,0,1:T(2,128)(2,1)S(1)} fusion(bf16[8,64,2048]{2,1,0:T(8,128)(2,1)} %all-gather.8.cloned.1.call-done, s32[2]{0:T(128)S(1)} %bitcast.87), kind=kOutput, calls=%fused_computation.8 | convolution fusion | flops 4456464 | bytes 2621448 | tf_op jit(solution)/shard_map/sm,mkc->skc/dot_general | solution.py:25
  50.9 0.4 convolution_bitcast_fusion.2
  51.3 14.5 %all-gather.4.cloned.1.call-done = bf16[8,64,2048]{2,1,0:T(8,128)(2,1)} async-done(((bf16[2,64,2048]{2,1,0:T(8,128)(2,1)}), bf16[8,64,2048]{2,1,0:T(8,128)(2,1)}) %all-gather.4.cloned.1.call-update) | async-done | bytes 2097168 | tf_op jit(solution)/shard_map/all_gather | solution.py:57
  65.8 3.1 %convolution_convert_fusion.2 = bf16[2,64,2048]{2,0,1:T(2,128)(2,1)S(1)} fusion(bf16[8,64,2048]{2,1,0:T(8,128)(2,1)} %all-gather.4.cloned.1.call-done, s32[2]{0:T(128)S(1)} %bitcast.88), kind=kOutput, calls=%fused_computation.10 | convolution fusion | flops 4456464 | bytes 2621448 | tf_op jit(solution)/shard_map/sm,mkc->skc/dot_general | solution.py:25
  69.0 0.4 convolution_bitcast_fusion.3
  69.4 21.2 %all-reduce.2 = (bf16[128,2,64]{0,2,1:T(8,128)(2,1)S(1)}, bf16[128,2,64]{0,2,1:T(8,128)(2,1)S(1)}) all-reduce(f32[128,2,64]{0,2,1:T(8,128)S(1)} %convolution_bitcast_fusion.3, f32[128,2,64]{0,2,1:T(8,128)S(1)} %convolution_bitcast_fusion.2), channel_id=1, replica_groups=mesh['ctx'=2,'req'=4,'mp'=4] {'mp'}, use_global_device_ids=true, to_apply=%region_0.0 | all-reduce | flops 32768 | bytes 196608 | tf_op jit(solution)/shard_map/psum | solution.py:65
  90.5 0.2 fusion.15
  90.8 6.4 %all_gather.31 = bf16[256,768]{0,1:T(8,128)(2,1)S(1)} all-gather(bf16[128,768]{0,1:T(8,128)(2,1)S(1)} %pad_maximum_fusion), channel_id=1, replica_groups=mesh['ctx'=2,'req'=4,'mp'=4] {'ctx'}, dimensions={0}, use_global_device_ids=true | all-gather | bytes 589824 | tf_op jit(solution)/shard_map/all_gather | solution.py:126
  97.2 0.0 all-gather.6.cloned.1.call-done
  97.2 3.2 %convolution_convert_fusion.1 = bf16[2,64,2048]{2,0,1:T(2,128)(2,1)S(1)} fusion(bf16[8,64,2048]{2,1,0:T(8,128)(2,1)} %all-gather.6.cloned.1.call-done, s32[2]{0:T(128)S(1)} %bitcast.89), kind=kOutput, calls=%fused_computation.9 | convolution fusion | flops 4456464 | bytes 2621448 | tf_op jit(solution)/shard_map/sm,mkc->skc/dot_general | solution.py:25
  100.5 0.6 fusion.4
  101.1 0.8 fusion
  101.9 1.3 %fusion.1 = (f32[2,2,8,128]{3,2,0,1:T(8,128)S(1)}, bf16[2,2,8,128,256]{3,4,2,0,1:T(8,128)(2,1)S(1)}) fusion(f32[2,256,128,2,8]{2,1,4,3,0:T(8,128)S(1)} %get-tuple-element.40, f32[2,2,8,128]{3,2,0,1:T(8,128)S(1)} %get-tuple-element.28, pred[128,256]{0,1:T(8,128)(4,1)S(1)} %fusion.24), kind=kLoop, calls=%fused_computation.3 | loop fusion | flops 6287360 | bytes 6356992 | tf_op jit(solution)/shard_map/while/body/eval_jaxpr/reduce_sum | solution.py:101
  103.2 0.5 fusion.6
  103.7 1.3 %copy.44 = bf16[2,1,128,2048]{3,2,1,0:T(8,128)(2,1)} copy(bf16[2,1,128,2048]{2,3,0,1:T(8,128)(2,1)S(1)} %bitcast.82) | data formatting | bytes 2097152 | tf_op jit(solution)/shard_map/convert_element_type | solution.py:146
  (26 shorter events, 0.1 us)
Async XLA Ops:
  6.5 44.4 %copy-start = (bf16[1,128,2048]{2,1,0:T(8,128)(2,1)S(1)}, bf16[1,128,2048]{2,1,0:T(8,128)(2,1)}, u32[]{:S(2)}) copy-start(bf16[1,128,2048]{2,1,0:T(8,128)(2,1)} %param.10) | copy-start | bytes 1572868
  6.5 20.7 %copy-start.3 = (bf16[2,32,2048]{2,1,0:T(8,128)(2,1)S(1)}, bf16[2,32,2048]{2,1,0:T(8,128)(2,1)}, u32[]{:S(2)}) copy-start(bf16[2,32,2048]{2,1,0:T(8,128)(2,1)} %param.15) | copy-start | bytes 786436
  6.5 29.2 %copy-start.5 = (bf16[1,128,256]{2,1,0:T(8,128)(2,1)S(1)}, bf16[1,128,256]{2,1,0:T(8,128)(2,1)}, u32[]{:S(2)}) copy-start(bf16[1,128,256]{2,1,0:T(8,128)(2,1)} %param.12) | copy-start | bytes 196612
  6.5 29.3 %copy-start.4 = (bf16[1,128,256]{2,1,0:T(8,128)(2,1)S(1)}, bf16[1,128,256]{2,1,0:T(8,128)(2,1)}, u32[]{:S(2)}) copy-start(bf16[1,128,256]{2,1,0:T(8,128)(2,1)} %param.13) | copy-start | bytes 196612
  6.5 29.5 %copy-start.2 = (bf16[1,128,2048]{2,1,0:T(8,128)(2,1)S(1)}, bf16[1,128,2048]{2,1,0:T(8,128)(2,1)}, u32[]{:S(2)}) copy-start(bf16[1,128,2048]{2,1,0:T(8,128)(2,1)} %param.11) | copy-start | bytes 1572868
  6.5 41.2 %all-gather.8.cloned.1.call-start = ((), (), s32[]{:S(2)}) async-start(), calls=%async_computation.2 | async-start | bytes 2621440 | tf_op jit(solution)/shard_map/all_gather | solution.py:55
  18.6 47.2 %all-gather.4.cloned.1.call-start = ((), (), s32[]{:S(2)}) async-start(), calls=%async_computation | async-start | bytes 2621440 | tf_op jit(solution)/shard_map/all_gather | solution.py:57
  27.2 70.1 %all-gather.6.cloned.1.call-start = ((), (), s32[]{:S(2)}) async-start(), calls=%async_computation.1 | async-start | bytes 2621440 | tf_op jit(solution)/shard_map/all_gather | solution.py:56
  35.9 0.8 copy-start.6
  36.0 11.3 %copy-start.7 = (s32[1,2]{1,0:T(1,128)S(1)}, s32[1,2]{1,0:T(1,128)}, u32[]{:S(2)}) copy-start(s32[1,2]{1,0:T(1,128)} %param.18) | copy-start | bytes 28
  97.2 3.9 %copy-start.1 = (bf16[256,768]{0,1:T(8,128)(2,1)}, bf16[256,768]{0,1:T(8,128)(2,1)S(1)}, u32[]{:S(2)}) copy-start(bf16[256,768]{0,1:T(8,128)(2,1)S(1)} %all_gather.31) | copy-start | bytes 1179652
  101.9 1.3 %slice-start = ((bf16[256,768]{0,1:T(8,128)(2,1)}), bf16[256,512]{0,1:T(8,128)(2,1)S(1)}, s32[]{:S(2)}) async-start(bf16[256,768]{0,1:T(8,128)(2,1)} %copy-done.1), calls=%async_computation.3 | async-start | bytes 524288 | tf_op jit(solution)/shard_map/split | solution.py:125
Sparse Core Ops, SparseCore 0:
  18.8 22.8 all-gather.7
  43.2 22.5 all-gather.3
  67.4 22.5 all-gather.5
